TPU v7x, 512 devices: a whole 4x4x16 slice. The times are simulated.
512 devices in a mesh: sub: 128 (over z, x, core), crow: 4 (over y).
Axes of the slice: x: 4, y: 4, z: 16, core: 2. Of those that a mesh axis runs over, the one named last changes fastest.
Arguments:
- deflation: bfloat16 [128, 12288, 128], P('sub', 'crow'), as said below
- diag_op: bfloat16 [128, 96, 128, 128], P('sub', 'crow'), as said below
- upper_op: bfloat16 [128, 96, 128, 128], P('sub', 'crow'), may hold values from -0.022094727 to 0.022094727
- tile_blocks: int32 [128, 4, 16], P('sub', 'crow'), may hold values from 0 to 23
- pair_counts: int32 [128, 8], P('sub'), may hold values from 0 to 8, as said below
- pivot_owner: int32 [128], P('sub'), may hold values from 0 to 3
Outputs:
- schur_self: float32 [16384, 128], P(('sub', 'crow'))
- schur_coupling: float32 [16384, 1024], P(('sub', 'crow'))
- panel: float32 [16384, 32], P(('sub', 'crow'))
Inputs may be any that keep to these rules, and one draw needn't show every extreme that they name: deflation has independent columns of different scales. Each diag_op block is symmetric with a positive diagonal, and every A_s is symmetric positive definite. pair_counts[s, j] equals pair_counts[s + o[j], 7 - j], is 0 where s + o[j] lies outside 0 to 127, and the pair of subdomains 0 and 1 shares 8 tiles.
All inputs are finite; a program needn't handle non-finite values.
Results may differ from a plain program's by a relative error of at most 0.0029.
Values may be sent and summed in bfloat16 or wider, within the bound.
No kernel may reach another device: no remote copies, remote signals or barrier semaphores. Data moves between devices by JAX's collectives and lax.ppermute only.
A program may use at most 64 MiB of HBM per device.

v0:
```python
import jax
import jax.numpy as jnp
from jax import lax
from jax.sharding import PartitionSpec as P


def padded_2(block, sides, width):
    for axis, dim in sides:
        count = lax.axis_size(axis)
        forward = [(i, i + 1) for i in range(count - 1)]
        backward = [(target, source) for source, target in forward]
        low = lax.ppermute(
            lax.slice_in_dim(block, block.shape[dim] - width, None, axis=dim), axis, forward
        )
        high = lax.ppermute(lax.slice_in_dim(block, 0, width, axis=dim), axis, backward)
        block = jnp.concatenate([low, block, high], axis=dim)
    return block


def shifted(value, axis, steps):
    count = lax.axis_size(axis)
    initial, last = (max(0, -steps), min(count, count - steps))
    return lax.ppermute(value, axis, [(source, source + steps) for source in range(initial, last)])


def broadcast(shard, axis, root):
    mine = lax.axis_index(axis) == root
    return lax.psum(jnp.where(mine, shard, jnp.zeros_like(shard)), axis)


def neighbour_offsets(across):
    return [-across - 1, -across, -across + 1, -1, 1, across - 1, across, across + 1]


def per_device(deflation, diag_op, upper_op, tile_blocks, pair_counts, pivot_owner):
    crow_count = lax.axis_size("crow")
    crow_place = lax.axis_index("crow")
    sub_count = lax.axis_size("sub")
    across = min(16, sub_count // 2)
    offsets = neighbour_offsets(across)
    local_rows = deflation[0]
    blocks_here, tile_rows = (diag_op.shape[1], diag_op.shape[2])
    coarse_width = local_rows.shape[1]
    slot_count = pair_counts.shape[1]
    per_slot = tile_blocks.shape[2] // slot_count
    padded = padded_2(local_rows, (("crow", 0),), tile_rows)
    stacked = padded.reshape(blocks_here + 2, tile_rows, coarse_width)
    centre = stacked[1:-1]
    previous_upper = shifted(upper_op[0, blocks_here - 1], "crow", 1)
    lower_blocks = jnp.concatenate([previous_upper[None], upper_op[0, :-1]], 0)
    product = (
        jnp.einsum("bij,bjk->bik", diag_op[0], centre, preferred_element_type=jnp.float32)
        + jnp.einsum("bij,bjk->bik", upper_op[0], stacked[2:], preferred_element_type=jnp.float32)
        + jnp.einsum("bji,bjk->bik", lower_blocks, stacked[:-2], preferred_element_type=jnp.float32)
    )
    applied = product.astype(jnp.bfloat16)
    chosen = tile_blocks[0, 0]
    own_tiles = centre[chosen].reshape(slot_count, per_slot, tile_rows, coarse_width)
    outgoing = applied[chosen].reshape(slot_count, per_slot, tile_rows, coarse_width)
    position = crow_place * per_slot + jnp.arange(per_slot, dtype=jnp.int32)
    live_mask = (position[None, :] < pair_counts[0][:, None]).astype(jnp.bfloat16)
    own_masked = own_tiles * live_mask[:, :, None, None]
    arrived = [None] * slot_count
    for slot_index in range(slot_count):
        arrived[slot_index] = shifted(
            outgoing[slot_count - 1 - slot_index], "sub", -offsets[slot_index]
        )
    received = jnp.stack(arrived)
    flat_vectors = centre.reshape(blocks_here * tile_rows, coarse_width)
    flat_applied = applied.reshape(blocks_here * tile_rows, coarse_width)
    row_share = coarse_width // crow_count
    owner_index = pivot_owner[0]
    gram_part = jnp.einsum(
        "nr,nk->rk", flat_vectors, flat_applied, preferred_element_type=jnp.float32
    )
    coupling = jnp.einsum(
        "jutr,jutk->rjk", own_masked, received, preferred_element_type=jnp.float32
    )
    own_rows = lax.psum_scatter(
        jnp.concatenate([gram_part[:, None, :], coupling], 1).reshape(
            row_share * lax.axis_size("crow"), (slot_count + 1) * coarse_width
        ),
        "crow",
        scatter_dimension=0,
        tiled=True,
    )
    leading = broadcast(own_rows, "crow", owner_index)
    pivot_block = lax.dynamic_slice_in_dim(leading, owner_index * row_share, row_share, 1)
    factor = jnp.linalg.cholesky(pivot_block)
    solved = jax.scipy.linalg.solve_triangular(factor, leading, lower=True)
    columns = lax.dynamic_slice_in_dim(own_rows, owner_index * row_share, row_share, 1)
    panel_rows = jax.scipy.linalg.solve_triangular(factor, columns.T, lower=True).T
    updated = own_rows - jnp.dot(panel_rows, solved, precision=lax.Precision.HIGHEST)
    return (updated[:, :coarse_width], updated[:, coarse_width:], panel_rows)


def solution(mesh):
    placed = (
        P("sub", "crow", None),
        P("sub", "crow", None, None),
        P("sub", "crow", None, None),
        P("sub", "crow", None),
        P("sub", None),
        P("sub"),
    )
    return jax.shard_map(
        per_device,
        mesh=mesh,
        in_specs=placed,
        out_specs=(P(("sub", "crow"), None), P(("sub", "crow"), None), P(("sub", "crow"), None)),
        check_vma=False,
    )
```

profile of v0, /device:TPU:2, one launch (start us, length us, event | category | flops | bytes accessed | tf_op | source)
XLA Modules:
  0.0 182.8 jit_solution(14846364270615309179)
XLA Ops:
  8.1 1.3 collective-permute-start
  9.4 4.5 %collective-permute-start.2 = (bf16[128,128]{1,0:T(8,128)(2,1)S(1)}, bf16[128,128]{1,0:T(8,128)(2,1)S(1)}, u32[]{:S(2)}, u32[]{:S(2)}) collective-permute-start(bf16[128,128]{1,0:T(8,128)(2,1)S(1)} %get-tuple-element.11), channel_id=1, source_target_pairs={{0,1},{1,2},{2,3},{4,5},{5,6},{6,7},{8,9},{9,10},{10,11},{12,13},{... | collective-permute-start | bytes 98312 | tf_op jit(solution)/shard_map/ppermute | solution.py:12
  14.8 3.5 %collective-permute-start.1 = (bf16[128,128]{0,1:T(8,128)(2,1)S(1)}, bf16[128,128]{0,1:T(8,128)(2,1)S(1)}, u32[]{:S(2)}, u32[]{:S(2)}) collective-permute-start(bf16[128,128]{0,1:T(8,128)(2,1)S(1)} %bitcast.93), channel_id=1, source_target_pairs={{0,1},{1,2},{2,3},{4,5},{5,6},{6,7},{8,9},{9,10},{10,11},{12,13},{... | collective-permute-start | bytes 98312 | tf_op jit(solution)/shard_map/ppermute | solution.py:23
  19.0 1.6 fusion.7
  21.6 2.3 %copy.28 = bf16[1,23,128,128]{2,3,1,0:T(8,128)(2,1)} copy(bf16[1,23,128,128]{3,2,1,0:T(8,128)(2,1)} %slice.98) | data formatting | bytes 1507328
  23.9 1.4 gather_fusion.1
  27.6 1.4 fusion.1
  29.0 1.9 %gather_fusion = bf16[16,128,128]{2,1,0:T(8,128)(2,1)S(1)} fusion(bf16[24,128,128]{2,1,0:T(8,128)(2,1)} %fusion.1, s32[1024]{0:T(1024)S(1)} %pad_clamp_fusion), kind=kCustom, calls=%fused_computation | custom fusion | bytes 1048640 | tf_op jit(solution)/shard_map/gather | solution.py:59
  30.9 3.9 %collective-permute-start.3 = (bf16[2,128,128]{2,1,0:T(8,128)(2,1)S(1)}, bf16[2,128,128]{2,1,0:T(8,128)(2,1)S(1)}, u32[]{:S(2)}, u32[]{:S(2)}) collective-permute-start(bf16[2,128,128]{2,1,0:T(8,128)(2,1)S(1)} %get-tuple-element.20), channel_id=1, source_target_pairs={{0,68},{4,72},{8,76},{12,80},{16,84},{20,88},{24,92},{28,96},{32,1... | collective-permute-start | bytes 196616 | tf_op jit(solution)/shard_map/ppermute | solution.py:23
  34.8 6.4 %collective-permute-start.4 = (bf16[2,128,128]{2,1,0:T(8,128)(2,1)S(1)}, bf16[2,128,128]{2,1,0:T(8,128)(2,1)S(1)}, u32[]{:S(2)}, u32[]{:S(2)}) collective-permute-start(bf16[2,128,128]{2,1,0:T(8,128)(2,1)S(1)} %get-tuple-element.19), channel_id=1, source_target_pairs={{0,64},{4,68},{8,72},{12,76},{16,80},{20,84},{24,88},{28,92},{32,9... | collective-permute-start | bytes 196616 | tf_op jit(solution)/shard_map/ppermute | solution.py:23
  41.2 6.9 %collective-permute-start.5 = (bf16[2,128,128]{2,1,0:T(8,128)(2,1)S(1)}, bf16[2,128,128]{2,1,0:T(8,128)(2,1)S(1)}, u32[]{:S(2)}, u32[]{:S(2)}) collective-permute-start(bf16[2,128,128]{2,1,0:T(8,128)(2,1)S(1)} %get-tuple-element.18), channel_id=1, source_target_pairs={{0,60},{4,64},{8,68},{12,72},{16,76},{20,80},{24,84},{28,88},{32,9... | collective-permute-start | bytes 196616 | tf_op jit(solution)/shard_map/ppermute | solution.py:23
  48.1 1.9 %collective-permute-start.6 = (bf16[2,128,128]{2,1,0:T(8,128)(2,1)S(1)}, bf16[2,128,128]{2,1,0:T(8,128)(2,1)S(1)}, u32[]{:S(2)}, u32[]{:S(2)}) collective-permute-start(bf16[2,128,128]{2,1,0:T(8,128)(2,1)S(1)} %get-tuple-element.17), channel_id=1, source_target_pairs={{0,4},{4,8},{8,12},{12,16},{16,20},{20,24},{24,28},{28,32},{32,36}... | collective-permute-start | bytes 196616 | tf_op jit(solution)/shard_map/ppermute | solution.py:23
  50.1 3.6 %collective-permute-start.7 = (bf16[2,128,128]{2,1,0:T(8,128)(2,1)S(1)}, bf16[2,128,128]{2,1,0:T(8,128)(2,1)S(1)}, u32[]{:S(2)}, u32[]{:S(2)}) collective-permute-start(bf16[2,128,128]{2,1,0:T(8,128)(2,1)S(1)} %get-tuple-element.16), channel_id=1, source_target_pairs={{4,0},{8,4},{12,8},{16,12},{20,16},{24,20},{28,24},{32,28},{36,32}... | collective-permute-start | bytes 196616 | tf_op jit(solution)/shard_map/ppermute | solution.py:23
  54.2 1.3 collective-permute-start.8
  55.5 1.3 collective-permute-start.9
  56.8 1.3 collective-permute-start.10
  58.2 3.9 %collective-permute-done.8 = bf16[2,128,128]{2,1,0:T(8,128)(2,1)S(1)} collective-permute-done((bf16[2,128,128]{2,1,0:T(8,128)(2,1)S(1)}, bf16[2,128,128]{2,1,0:T(8,128)(2,1)S(1)}, u32[]{:S(2)}, u32[]{:S(2)}) %collective-permute-start.8) | collective-permute-done | bytes 65568 | tf_op jit(solution)/shard_map/ppermute | solution.py:23
  62.1 6.8 %collective-permute-done.9 = bf16[2,128,128]{2,1,0:T(8,128)(2,1)S(1)} collective-permute-done((bf16[2,128,128]{2,1,0:T(8,128)(2,1)S(1)}, bf16[2,128,128]{2,1,0:T(8,128)(2,1)S(1)}, u32[]{:S(2)}, u32[]{:S(2)}) %collective-permute-start.9) | collective-permute-done | bytes 65568 | tf_op jit(solution)/shard_map/ppermute | solution.py:23
  71.6 30.8 %reduce-scatter.4.cloned.1.call-done = f32[32,1152]{1,0:T(8,128)} async-done(((f32[128,1152]{1,0:T(8,128)}), f32[32,1152]{1,0:T(8,128)}) %reduce-scatter.4.cloned.1.call-update) | async-done | bytes 147472 | tf_op jit(solution)/shard_map/reduce_scatter | solution.py:79
  102.4 1.2 copy.26
  104.5 58.9 %all-reduce.2.cloned.1.call-done = f32[32,1152]{0,1:T(8,128)} async-done(((f32[32,1152]{0,1:T(8,128)}), f32[32,1152]{0,1:T(8,128)}) %all-reduce.2.cloned.1.call-update) | async-done | bytes 147472 | tf_op jit(solution)/shard_map/psum | solution.py:28
  164.9 2.9 %cholesky.16 = f32[32,32]{1,0:T(8,128)S(1)} custom-call(f32[32,32]{1,0:T(8,128)S(1)} %fusion.16), custom_call_target="Cholesky" | custom-call | tf_op jit(solution)/shard_map/jit(cholesky)/cholesky | solution.py:89
  169.2 2.4 %custom-call.10 = f32[1,32,32]{1,2,0:T(8,128)S(1)} custom-call(f32[1,32,32]{2,1,0:T(8,128)S(1)} %fusion.11), custom_call_target="InvertDiagBlocksLowerTriangular" | custom-call | tf_op jit(solution)/shard_map/jit(_solve_triangular)/triangular_solve | solution.py:92
  171.9 1.8 fusion.12
  (66 shorter events, 14.5 us)
Async XLA Ops:
  7.2 11.8 %copy-start = (bf16[1,24,128,128]{3,2,1,0:T(8,128)(2,1)S(1)}, bf16[1,24,128,128]{3,2,1,0:T(8,128)(2,1)}, u32[]{:S(2)}) copy-start(bf16[1,24,128,128]{3,2,1,0:T(8,128)(2,1)} %param.7) | copy-start | bytes 2359300
  7.2 95.2 %reduce-scatter.4.cloned.1.call-start = ((), (), s32[]{:S(2)}) async-start(), calls=%async_computation.2 | async-start | bytes 737280 | tf_op jit(solution)/shard_map/reduce_scatter | solution.py:79
  8.1 17.3 %collective-permute-start = (bf16[128,128]{1,0:T(8,128)(2,1)S(1)}, bf16[128,128]{1,0:T(8,128)(2,1)S(1)}, u32[]{:S(2)}, u32[]{:S(2)}) collective-permute-start(bf16[128,128]{1,0:T(8,128)(2,1)S(1)} %get-tuple-element.12), channel_id=1, source_target_pairs={{1,0},{2,1},{3,2},{5,4},{6,5},{7,6},{9,8},{10,9},{11,10},{13,12},{... | collective-permute-start | bytes 98312 | tf_op jit(solution)/shard_map/ppermute | solution.py:15
  9.4 16.0 %collective-permute-start.2 = (bf16[128,128]{1,0:T(8,128)(2,1)S(1)}, bf16[128,128]{1,0:T(8,128)(2,1)S(1)}, u32[]{:S(2)}, u32[]{:S(2)}) collective-permute-start(bf16[128,128]{1,0:T(8,128)(2,1)S(1)} %get-tuple-element.11), channel_id=1, source_target_pairs={{0,1},{1,2},{2,3},{4,5},{5,6},{6,7},{8,9},{9,10},{10,11},{12,13},{... | collective-permute-start | bytes 98312 | tf_op jit(solution)/shard_map/ppermute | solution.py:12
  14.8 12.1 %collective-permute-start.1 = (bf16[128,128]{0,1:T(8,128)(2,1)S(1)}, bf16[128,128]{0,1:T(8,128)(2,1)S(1)}, u32[]{:S(2)}, u32[]{:S(2)}) collective-permute-start(bf16[128,128]{0,1:T(8,128)(2,1)S(1)} %bitcast.93), channel_id=1, source_target_pairs={{0,1},{1,2},{2,3},{4,5},{5,6},{6,7},{8,9},{9,10},{10,11},{12,13},{... | collective-permute-start | bytes 98312 | tf_op jit(solution)/shard_map/ppermute | solution.py:23
  19.0 1.6 copy-start.8
  19.0 1.7 copy-start.3
  20.5 3.4 %copy-start.1 = (bf16[1,3072,128]{2,1,0:T(8,128)(2,1)S(1)}, bf16[1,3072,128]{2,1,0:T(8,128)(2,1)}, u32[]{:S(2)}) copy-start(bf16[1,3072,128]{2,1,0:T(8,128)(2,1)} %param.6) | copy-start | bytes 2359300
  25.4 1.1 copy-start.4
  26.5 1.1 copy-start.5
  29.0 24.7 %copy-start.2 = (bf16[24,128,128]{2,1,0:T(8,128)(2,1)S(1)}, bf16[24,128,128]{2,1,0:T(8,128)(2,1)}, u32[]{:S(2)}) copy-start(bf16[24,128,128]{2,1,0:T(8,128)(2,1)} %fusion.1) | copy-start | bytes 2359300
  30.9 38.5 %copy-start.6 = (bf16[16,128,128]{2,1,0:T(8,128)(2,1)S(1)}, bf16[16,128,128]{2,1,0:T(8,128)(2,1)}, u32[]{:S(2)}) copy-start(bf16[16,128,128]{2,1,0:T(8,128)(2,1)} %gather_fusion.1) | copy-start | bytes 1572868
  30.9 23.2 %collective-permute-start.3 = (bf16[2,128,128]{2,1,0:T(8,128)(2,1)S(1)}, bf16[2,128,128]{2,1,0:T(8,128)(2,1)S(1)}, u32[]{:S(2)}, u32[]{:S(2)}) collective-permute-start(bf16[2,128,128]{2,1,0:T(8,128)(2,1)S(1)} %get-tuple-element.20), channel_id=1, source_target_pairs={{0,68},{4,72},{8,76},{12,80},{16,84},{20,88},{24,92},{28,96},{32,1... | collective-permute-start | bytes 196616 | tf_op jit(solution)/shard_map/ppermute | solution.py:23
  34.8 20.7 %collective-permute-start.4 = (bf16[2,128,128]{2,1,0:T(8,128)(2,1)S(1)}, bf16[2,128,128]{2,1,0:T(8,128)(2,1)S(1)}, u32[]{:S(2)}, u32[]{:S(2)}) collective-permute-start(bf16[2,128,128]{2,1,0:T(8,128)(2,1)S(1)} %get-tuple-element.19), channel_id=1, source_target_pairs={{0,64},{4,68},{8,72},{12,76},{16,80},{20,84},{24,88},{28,92},{32,9... | collective-permute-start | bytes 196616 | tf_op jit(solution)/shard_map/ppermute | solution.py:23
  41.2 15.6 %collective-permute-start.5 = (bf16[2,128,128]{2,1,0:T(8,128)(2,1)S(1)}, bf16[2,128,128]{2,1,0:T(8,128)(2,1)S(1)}, u32[]{:S(2)}, u32[]{:S(2)}) collective-permute-start(bf16[2,128,128]{2,1,0:T(8,128)(2,1)S(1)} %get-tuple-element.18), channel_id=1, source_target_pairs={{0,60},{4,64},{8,68},{12,72},{16,76},{20,80},{24,84},{28,88},{32,9... | collective-permute-start | bytes 196616 | tf_op jit(solution)/shard_map/ppermute | solution.py:23
  48.1 10.0 %collective-permute-start.6 = (bf16[2,128,128]{2,1,0:T(8,128)(2,1)S(1)}, bf16[2,128,128]{2,1,0:T(8,128)(2,1)S(1)}, u32[]{:S(2)}, u32[]{:S(2)}) collective-permute-start(bf16[2,128,128]{2,1,0:T(8,128)(2,1)S(1)} %get-tuple-element.17), channel_id=1, source_target_pairs={{0,4},{4,8},{8,12},{12,16},{16,20},{20,24},{24,28},{28,32},{32,36}... | collective-permute-start | bytes 196616 | tf_op jit(solution)/shard_map/ppermute | solution.py:23
  50.1 8.1 %collective-permute-start.7 = (bf16[2,128,128]{2,1,0:T(8,128)(2,1)S(1)}, bf16[2,128,128]{2,1,0:T(8,128)(2,1)S(1)}, u32[]{:S(2)}, u32[]{:S(2)}) collective-permute-start(bf16[2,128,128]{2,1,0:T(8,128)(2,1)S(1)} %get-tuple-element.16), channel_id=1, source_target_pairs={{4,0},{8,4},{12,8},{16,12},{20,16},{24,20},{28,24},{32,28},{36,32}... | collective-permute-start | bytes 196616 | tf_op jit(solution)/shard_map/ppermute | solution.py:23
  54.2 7.9 %collective-permute-start.8 = (bf16[2,128,128]{2,1,0:T(8,128)(2,1)S(1)}, bf16[2,128,128]{2,1,0:T(8,128)(2,1)S(1)}, u32[]{:S(2)}, u32[]{:S(2)}) collective-permute-start(bf16[2,128,128]{2,1,0:T(8,128)(2,1)S(1)} %get-tuple-element.15), channel_id=1, source_target_pairs={{60,0},{64,4},{68,8},{72,12},{76,16},{80,20},{84,24},{88,28},{92,3... | collective-permute-start | bytes 196616 | tf_op jit(solution)/shard_map/ppermute | solution.py:23
  55.5 13.4 %collective-permute-start.9 = (bf16[2,128,128]{2,1,0:T(8,128)(2,1)S(1)}, bf16[2,128,128]{2,1,0:T(8,128)(2,1)S(1)}, u32[]{:S(2)}, u32[]{:S(2)}) collective-permute-start(bf16[2,128,128]{2,1,0:T(8,128)(2,1)S(1)} %get-tuple-element.14), channel_id=1, source_target_pairs={{64,0},{68,4},{72,8},{76,12},{80,16},{84,20},{88,24},{92,28},{96,3... | collective-permute-start | bytes 196616 | tf_op jit(solution)/shard_map/ppermute | solution.py:23
  56.8 12.5 %collective-permute-start.10 = (bf16[2,128,128]{2,1,0:T(8,128)(2,1)S(1)}, bf16[2,128,128]{2,1,0:T(8,128)(2,1)S(1)}, u32[]{:S(2)}, u32[]{:S(2)}) collective-permute-start(bf16[2,128,128]{2,1,0:T(8,128)(2,1)S(1)} %get-tuple-element.13), channel_id=1, source_target_pairs={{68,0},{72,4},{76,8},{80,12},{84,16},{88,20},{92,24},{96,28},{100,... | collective-permute-start | bytes 196616 | tf_op jit(solution)/shard_map/ppermute | solution.py:23
  70.9 92.5 %all-reduce.2.cloned.1.call-start = ((), (), s32[]{:S(2)}) async-start(), calls=%async_computation.1 | async-start | bytes 1179648 | tf_op jit(solution)/shard_map/psum | solution.py:28
  102.4 71.3 %copy-start.7 = (f32[32,1152]{1,0:T(8,128)S(1)}, f32[32,1152]{1,0:T(8,128)}, u32[]{:S(2)}) copy-start(f32[32,1152]{1,0:T(8,128)} %reduce-scatter.4.cloned.1.call-done) | copy-start | bytes 442372
Sparse Core Ops, SparseCore 0:
  71.0 31.3 reduce-scatter.3
  104.7 58.6 all-reduce.1
where the time goes:
time: 184 us; the launch traced here: 183 us
  waiting for transfers between devices  101 us (55%)
  starting transfers between devices  36 us (20%)
  local copies, waits for them, and re-layouts  15.2 us (8%)
  between operations  15 us (8%)
  other arithmetic  9.15 us (5%)
  matrix products  6.45 us (4%)
    psum x1, waiting for transfers between devices, broadcast(): return lax.psum(jnp.where(mine, shard, jnp.zeros_like(shard)), axis)  58.9 us
    reduce_scatter x1, waiting for transfers between devices, per_device(): lax.psum_scatter(jnp.concatenate([gram_part[:, None, :], coupling], 1).re...  30.8 us
    ppermute x9, starting transfers between devices, shifted(): lax.ppermute(value, axis, [(source, source + steps) for source in range(i...  30.1 us
    ppermute x9, waiting for transfers between devices, shifted(): lax.ppermute(value, axis, [(source, source + steps) for source in range(i...  11.1 us
    unnamed x30, local copies, waits for them, and re-layouts  7.24 us
    ppermute x1, starting transfers between devices, padded_2(): lax.ppermute(lax.slice_in_dim(block, block.shape[dim] - width, None, axis...  4.55 us
  transfers between devices with their start and end apart: 13, of which 5 were waited for; matrix products, arithmetic and copies ran while one was open for 5% of the time, Pallas kernels for 0%

commit v1 on v0

--- a/solution.py
+++ b/solution.py
@@ -2,6 +2,8 @@
 import jax.numpy as jnp
 from jax import lax
 from jax.sharding import PartitionSpec as P
+
+remake_the_copies = lambda state, named_axis: jnp.sum(jax.lax.all_gather(state, named_axis), axis=0)
 
 
 def padded_2(block, sides, width):
@@ -25,7 +27,7 @@
 
 def broadcast(shard, axis, root):
     mine = lax.axis_index(axis) == root
-    return lax.psum(jnp.where(mine, shard, jnp.zeros_like(shard)), axis)
+    return remake_the_copies(jnp.where(mine, shard, jnp.zeros_like(shard)), axis)
 
 
 def neighbour_offsets(across):

time: 184 us -> 134 us (0.73)
  the two profiles are of different devices: /device:TPU:2 before, /device:TPU:4 now
where the time goes in v1:
time: 134 us; the launch traced here: 133 us
  waiting for transfers between devices  42 us (31%)
  starting transfers between devices  36 us (27%)
  between operations  15 us (11%)
  local copies, waits for them, and re-layouts  13.3 us (10%)
  blocking collectives  12.9 us (10%)
  other arithmetic  8.67 us (6%)
  matrix products  5.02 us (4%)
    reduce_scatter x1, waiting for transfers between devices, per_device(): lax.psum_scatter(jnp.concatenate([gram_part[:, None, :], coupling], 1).re...  31.2 us
    ppermute x9, starting transfers between devices, shifted(): lax.ppermute(value, axis, [(source, source + steps) for source in range(i...  30.1 us
    all_gather x1, blocking collectives, jax.lax.all_gather(state, named_axis)  12.9 us
    ppermute x9, waiting for transfers between devices, shifted(): lax.ppermute(value, axis, [(source, source + steps) for source in range(i...  10.8 us
    unnamed x29, local copies, waits for them, and re-layouts  5.03 us
    ppermute x1, starting transfers between devices, padded_2(): lax.ppermute(lax.slice_in_dim(block, block.shape[dim] - width, None, axis...  4.55 us
    another operation x3, other arithmetic, per_device(): factor = jnp.linalg.cholesky(pivot_block)  3.6 us
    another operation x2, other arithmetic, per_device(): jax.scipy.linalg.solve_triangular(factor, columns.T, lower=True)  3.09 us
  transfers between devices with their start and end apart: 12, of which 4 were waited for; matrix products, arithmetic and copies ran while one was open for 7% of the time, Pallas kernels for 0%

profile of v1, /device:TPU:4, one launch (start us, length us, event | category | flops | bytes accessed | tf_op | source)
XLA Modules:
  0.0 133.0 jit_solution(16932461411767773442)
XLA Ops:
  8.1 1.3 collective-permute-start
  9.4 4.5 %collective-permute-start.2 = (bf16[128,128]{1,0:T(8,128)(2,1)S(1)}, bf16[128,128]{1,0:T(8,128)(2,1)S(1)}, u32[]{:S(2)}, u32[]{:S(2)}) collective-permute-start(bf16[128,128]{1,0:T(8,128)(2,1)S(1)} %get-tuple-element.11), channel_id=1, source_target_pairs={{0,1},{1,2},{2,3},{4,5},{5,6},{6,7},{8,9},{9,10},{10,11},{12,13},{... | collective-permute-start | bytes 98312 | tf_op jit(solution)/shard_map/ppermute | solution.py:14
  14.8 3.5 %collective-permute-start.1 = (bf16[128,128]{0,1:T(8,128)(2,1)S(1)}, bf16[128,128]{0,1:T(8,128)(2,1)S(1)}, u32[]{:S(2)}, u32[]{:S(2)}) collective-permute-start(bf16[128,128]{0,1:T(8,128)(2,1)S(1)} %bitcast.94), channel_id=1, source_target_pairs={{0,1},{1,2},{2,3},{4,5},{5,6},{6,7},{8,9},{9,10},{10,11},{12,13},{... | collective-permute-start | bytes 98312 | tf_op jit(solution)/shard_map/ppermute | solution.py:25
  19.0 1.6 %fusion.7 = f32[24,128,128]{2,1,0:T(8,128)S(1)} fusion(bf16[24,128,128]{2,1,0:T(8,128)(2,1)} %bitcast.82, bf16[1,24,128,128]{3,2,1,0:T(8,128)(2,1)S(1)} %copy-done), kind=kOutput, calls=%fused_computation.15 | convolution fusion | flops 100663296 | bytes 3145728 | tf_op jit(solution)/shard_map/bij,bjk->bik/dot_general | solution.py:54
  21.6 2.3 %copy.25 = bf16[1,23,128,128]{2,3,1,0:T(8,128)(2,1)} copy(bf16[1,23,128,128]{3,2,1,0:T(8,128)(2,1)} %slice.98) | data formatting | bytes 1507328
  23.9 1.4 %gather_fusion.1 = bf16[16,128,128]{2,1,0:T(8,128)(2,1)} fusion(bf16[24,128,128]{2,1,0:T(8,128)(2,1)S(1)} %bitcast.83, s32[1024]{0:T(1024)S(1)} %pad_clamp_fusion), kind=kCustom, calls=%fused_computation.1 | custom fusion | bytes 1048640 | tf_op jit(solution)/shard_map/gather | solution.py:60
  25.4 1.0 copy-done.4
  27.6 1.4 %fusion.1 = bf16[24,128,128]{2,1,0:T(8,128)(2,1)} fusion(f32[24,128,128]{2,1,0:T(8,128)S(1)} %fusion.7, f32[24,128,128]{1,2,0:T(8,128)S(1)} %fusion.5, bf16[24,128,128]{2,1,0:T(8,128)(2,1)S(1)} %bitcast.87, bf16[23,128,128]{1,2,0:T(8,128)(2,1)S(1)} %bitcast.88, bf16[1,128,128]{1,2,0:T(8,128)(2,1)S(1)} %bitcast.93), kind=kOutput, calls=%fused_computation.5 | convolution fusion | flops 102236160 | bytes 5505024 | tf_op jit(solution)/shard_map/bji,bjk->bik/dot_general | solution.py:56
  29.0 1.9 %gather_fusion = bf16[16,128,128]{2,1,0:T(8,128)(2,1)S(1)} fusion(bf16[24,128,128]{2,1,0:T(8,128)(2,1)} %fusion.1, s32[1024]{0:T(1024)S(1)} %pad_clamp_fusion), kind=kCustom, calls=%fused_computation | custom fusion | bytes 1048640 | tf_op jit(solution)/shard_map/gather | solution.py:61
  30.9 3.9 %collective-permute-start.3 = (bf16[2,128,128]{2,1,0:T(8,128)(2,1)S(1)}, bf16[2,128,128]{2,1,0:T(8,128)(2,1)S(1)}, u32[]{:S(2)}, u32[]{:S(2)}) collective-permute-start(bf16[2,128,128]{2,1,0:T(8,128)(2,1)S(1)} %get-tuple-element.20), channel_id=1, source_target_pairs={{0,68},{4,72},{8,76},{12,80},{16,84},{20,88},{24,92},{28,96},{32,1... | collective-permute-start | bytes 196616 | tf_op jit(solution)/shard_map/ppermute | solution.py:25
  34.8 6.4 %collective-permute-start.4 = (bf16[2,128,128]{2,1,0:T(8,128)(2,1)S(1)}, bf16[2,128,128]{2,1,0:T(8,128)(2,1)S(1)}, u32[]{:S(2)}, u32[]{:S(2)}) collective-permute-start(bf16[2,128,128]{2,1,0:T(8,128)(2,1)S(1)} %get-tuple-element.19), channel_id=1, source_target_pairs={{0,64},{4,68},{8,72},{12,76},{16,80},{20,84},{24,88},{28,92},{32,9... | collective-permute-start | bytes 196616 | tf_op jit(solution)/shard_map/ppermute | solution.py:25
  41.2 6.9 %collective-permute-start.5 = (bf16[2,128,128]{2,1,0:T(8,128)(2,1)S(1)}, bf16[2,128,128]{2,1,0:T(8,128)(2,1)S(1)}, u32[]{:S(2)}, u32[]{:S(2)}) collective-permute-start(bf16[2,128,128]{2,1,0:T(8,128)(2,1)S(1)} %get-tuple-element.18), channel_id=1, source_target_pairs={{0,60},{4,64},{8,68},{12,72},{16,76},{20,80},{24,84},{28,88},{32,9... | collective-permute-start | bytes 196616 | tf_op jit(solution)/shard_map/ppermute | solution.py:25
  48.1 1.9 %collective-permute-start.6 = (bf16[2,128,128]{2,1,0:T(8,128)(2,1)S(1)}, bf16[2,128,128]{2,1,0:T(8,128)(2,1)S(1)}, u32[]{:S(2)}, u32[]{:S(2)}) collective-permute-start(bf16[2,128,128]{2,1,0:T(8,128)(2,1)S(1)} %get-tuple-element.17), channel_id=1, source_target_pairs={{0,4},{4,8},{8,12},{12,16},{16,20},{20,24},{24,28},{28,32},{32,36}... | collective-permute-start | bytes 196616 | tf_op jit(solution)/shard_map/ppermute | solution.py:25
  50.1 3.6 %collective-permute-start.7 = (bf16[2,128,128]{2,1,0:T(8,128)(2,1)S(1)}, bf16[2,128,128]{2,1,0:T(8,128)(2,1)S(1)}, u32[]{:S(2)}, u32[]{:S(2)}) collective-permute-start(bf16[2,128,128]{2,1,0:T(8,128)(2,1)S(1)} %get-tuple-element.16), channel_id=1, source_target_pairs={{4,0},{8,4},{12,8},{16,12},{20,16},{24,20},{28,24},{32,28},{36,32}... | collective-permute-start | bytes 196616 | tf_op jit(solution)/shard_map/ppermute | solution.py:25
  54.1 1.3 collective-permute-start.8
  55.5 1.3 collective-permute-start.9
  56.8 1.3 collective-permute-start.10
  58.2 3.8 %collective-permute-done.8 = bf16[2,128,128]{2,1,0:T(8,128)(2,1)S(1)} collective-permute-done((bf16[2,128,128]{2,1,0:T(8,128)(2,1)S(1)}, bf16[2,128,128]{2,1,0:T(8,128)(2,1)S(1)}, u32[]{:S(2)}, u32[]{:S(2)}) %collective-permute-start.8) | collective-permute-done | bytes 65568 | tf_op jit(solution)/shard_map/ppermute | solution.py:25
  61.9 6.9 %collective-permute-done.9 = bf16[2,128,128]{2,1,0:T(8,128)(2,1)S(1)} collective-permute-done((bf16[2,128,128]{2,1,0:T(8,128)(2,1)S(1)}, bf16[2,128,128]{2,1,0:T(8,128)(2,1)S(1)}, u32[]{:S(2)}, u32[]{:S(2)}) %collective-permute-start.9) | collective-permute-done | bytes 65568 | tf_op jit(solution)/shard_map/ppermute | solution.py:25
  69.5 1.1 copy.18
  71.2 31.2 %reduce-scatter.2.cloned.1.call-done = f32[32,1152]{1,0:T(8,128)} async-done(((f32[128,1152]{1,0:T(8,128)}), f32[32,1152]{1,0:T(8,128)}) %reduce-scatter.2.cloned.1.call-update) | async-done | bytes 147472 | tf_op jit(solution)/shard_map/reduce_scatter | solution.py:81
  103.4 12.9 %all-gather = f32[128,1152]{1,0:T(8,128)S(1)} all-gather(f32[32,1152]{1,0:T(8,128)S(1)} %broadcast_select_fusion), channel_id=2, replica_groups=mesh['sub'=128,'crow'=4] {'crow'}, dimensions={0}, use_global_device_ids=true | all-gather | bytes 737280 | tf_op jit(solution)/shard_map/all_gather | solution.py:6
  116.6 2.9 %cholesky.16 = f32[32,32]{1,0:T(8,128)S(1)} custom-call(f32[32,32]{1,0:T(8,128)S(1)} %fusion.16), custom_call_target="Cholesky" | custom-call | tf_op jit(solution)/shard_map/jit(cholesky)/cholesky | solution.py:91
  120.9 2.4 %custom-call.10 = f32[1,32,32]{1,2,0:T(8,128)S(1)} custom-call(f32[1,32,32]{2,1,0:T(8,128)S(1)} %fusion.11), custom_call_target="InvertDiagBlocksLowerTriangular" | custom-call | tf_op jit(solution)/shard_map/jit(_solve_triangular)/triangular_solve | solution.py:94
  (64 shorter events, 11.3 us)
Async XLA Ops:
  7.2 11.8 %copy-start = (bf16[1,24,128,128]{3,2,1,0:T(8,128)(2,1)S(1)}, bf16[1,24,128,128]{3,2,1,0:T(8,128)(2,1)}, u32[]{:S(2)}) copy-start(bf16[1,24,128,128]{3,2,1,0:T(8,128)(2,1)} %param.7) | copy-start | bytes 2359300
  7.2 95.2 %reduce-scatter.2.cloned.1.call-start = ((), (), s32[]{:S(2)}) async-start(), calls=%async_computation.1 | async-start | bytes 737280 | tf_op jit(solution)/shard_map/reduce_scatter | solution.py:81
  8.1 17.3 %collective-permute-start = (bf16[128,128]{1,0:T(8,128)(2,1)S(1)}, bf16[128,128]{1,0:T(8,128)(2,1)S(1)}, u32[]{:S(2)}, u32[]{:S(2)}) collective-permute-start(bf16[128,128]{1,0:T(8,128)(2,1)S(1)} %get-tuple-element.12), channel_id=1, source_target_pairs={{1,0},{2,1},{3,2},{5,4},{6,5},{7,6},{9,8},{10,9},{11,10},{13,12},{... | collective-permute-start | bytes 98312 | tf_op jit(solution)/shard_map/ppermute | solution.py:17
  9.4 16.0 %collective-permute-start.2 = (bf16[128,128]{1,0:T(8,128)(2,1)S(1)}, bf16[128,128]{1,0:T(8,128)(2,1)S(1)}, u32[]{:S(2)}, u32[]{:S(2)}) collective-permute-start(bf16[128,128]{1,0:T(8,128)(2,1)S(1)} %get-tuple-element.11), channel_id=1, source_target_pairs={{0,1},{1,2},{2,3},{4,5},{5,6},{6,7},{8,9},{9,10},{10,11},{12,13},{... | collective-permute-start | bytes 98312 | tf_op jit(solution)/shard_map/ppermute | solution.py:14
  14.8 12.0 %collective-permute-start.1 = (bf16[128,128]{0,1:T(8,128)(2,1)S(1)}, bf16[128,128]{0,1:T(8,128)(2,1)S(1)}, u32[]{:S(2)}, u32[]{:S(2)}) collective-permute-start(bf16[128,128]{0,1:T(8,128)(2,1)S(1)} %bitcast.94), channel_id=1, source_target_pairs={{0,1},{1,2},{2,3},{4,5},{5,6},{6,7},{8,9},{9,10},{10,11},{12,13},{... | collective-permute-start | bytes 98312 | tf_op jit(solution)/shard_map/ppermute | solution.py:25
  19.0 1.6 %copy-start.8 = (s32[1,8]{1,0:T(1,128)S(1)}, s32[1,8]{1,0:T(1,128)}, u32[]{:S(2)}) copy-start(s32[1,8]{1,0:T(1,128)} %param.10) | copy-start | bytes 100
  19.0 1.7 %copy-start.3 = (bf16[1,24,128,128]{3,2,1,0:T(8,128)(2,1)S(1)}, bf16[1,24,128,128]{3,2,1,0:T(8,128)(2,1)}, u32[]{:S(2)}) copy-start(bf16[1,24,128,128]{3,2,1,0:T(8,128)(2,1)} %param.8) | copy-start | bytes 2359300
  20.5 3.4 %copy-start.1 = (bf16[1,3072,128]{2,1,0:T(8,128)(2,1)S(1)}, bf16[1,3072,128]{2,1,0:T(8,128)(2,1)}, u32[]{:S(2)}) copy-start(bf16[1,3072,128]{2,1,0:T(8,128)(2,1)} %param.6) | copy-start | bytes 2359300
  25.3 1.1 copy-start.4
  26.5 1.1 copy-start.5
  29.0 24.7 %copy-start.2 = (bf16[24,128,128]{2,1,0:T(8,128)(2,1)S(1)}, bf16[24,128,128]{2,1,0:T(8,128)(2,1)}, u32[]{:S(2)}) copy-start(bf16[24,128,128]{2,1,0:T(8,128)(2,1)} %fusion.1) | copy-start | bytes 2359300
  30.9 38.1 %copy-start.6 = (bf16[16,128,128]{2,1,0:T(8,128)(2,1)S(1)}, bf16[16,128,128]{2,1,0:T(8,128)(2,1)}, u32[]{:S(2)}) copy-start(bf16[16,128,128]{2,1,0:T(8,128)(2,1)} %gather_fusion.1) | copy-start | bytes 1572868
  30.9 23.2 %collective-permute-start.3 = (bf16[2,128,128]{2,1,0:T(8,128)(2,1)S(1)}, bf16[2,128,128]{2,1,0:T(8,128)(2,1)S(1)}, u32[]{:S(2)}, u32[]{:S(2)}) collective-permute-start(bf16[2,128,128]{2,1,0:T(8,128)(2,1)S(1)} %get-tuple-element.20), channel_id=1, source_target_pairs={{0,68},{4,72},{8,76},{12,80},{16,84},{20,88},{24,92},{28,96},{32,1... | collective-permute-start | bytes 196616 | tf_op jit(solution)/shard_map/ppermute | solution.py:25
  34.8 20.6 %collective-permute-start.4 = (bf16[2,128,128]{2,1,0:T(8,128)(2,1)S(1)}, bf16[2,128,128]{2,1,0:T(8,128)(2,1)S(1)}, u32[]{:S(2)}, u32[]{:S(2)}) collective-permute-start(bf16[2,128,128]{2,1,0:T(8,128)(2,1)S(1)} %get-tuple-element.19), channel_id=1, source_target_pairs={{0,64},{4,68},{8,72},{12,76},{16,80},{20,84},{24,88},{28,92},{32,9... | collective-permute-start | bytes 196616 | tf_op jit(solution)/shard_map/ppermute | solution.py:25
  41.2 15.6 %collective-permute-start.5 = (bf16[2,128,128]{2,1,0:T(8,128)(2,1)S(1)}, bf16[2,128,128]{2,1,0:T(8,128)(2,1)S(1)}, u32[]{:S(2)}, u32[]{:S(2)}) collective-permute-start(bf16[2,128,128]{2,1,0:T(8,128)(2,1)S(1)} %get-tuple-element.18), channel_id=1, source_target_pairs={{0,60},{4,64},{8,68},{12,72},{16,76},{20,80},{24,84},{28,88},{32,9... | collective-permute-start | bytes 196616 | tf_op jit(solution)/shard_map/ppermute | solution.py:25
  48.1 10.0 %collective-permute-start.6 = (bf16[2,128,128]{2,1,0:T(8,128)(2,1)S(1)}, bf16[2,128,128]{2,1,0:T(8,128)(2,1)S(1)}, u32[]{:S(2)}, u32[]{:S(2)}) collective-permute-start(bf16[2,128,128]{2,1,0:T(8,128)(2,1)S(1)} %get-tuple-element.17), channel_id=1, source_target_pairs={{0,4},{4,8},{8,12},{12,16},{16,20},{20,24},{24,28},{28,32},{32,36}... | collective-permute-start | bytes 196616 | tf_op jit(solution)/shard_map/ppermute | solution.py:25
  50.1 8.1 %collective-permute-start.7 = (bf16[2,128,128]{2,1,0:T(8,128)(2,1)S(1)}, bf16[2,128,128]{2,1,0:T(8,128)(2,1)S(1)}, u32[]{:S(2)}, u32[]{:S(2)}) collective-permute-start(bf16[2,128,128]{2,1,0:T(8,128)(2,1)S(1)} %get-tuple-element.16), channel_id=1, source_target_pairs={{4,0},{8,4},{12,8},{16,12},{20,16},{24,20},{28,24},{32,28},{36,32}... | collective-permute-start | bytes 196616 | tf_op jit(solution)/shard_map/ppermute | solution.py:25
  54.1 7.8 %collective-permute-start.8 = (bf16[2,128,128]{2,1,0:T(8,128)(2,1)S(1)}, bf16[2,128,128]{2,1,0:T(8,128)(2,1)S(1)}, u32[]{:S(2)}, u32[]{:S(2)}) collective-permute-start(bf16[2,128,128]{2,1,0:T(8,128)(2,1)S(1)} %get-tuple-element.15), channel_id=1, source_target_pairs={{60,0},{64,4},{68,8},{72,12},{76,16},{80,20},{84,24},{88,28},{92,3... | collective-permute-start | bytes 196616 | tf_op jit(solution)/shard_map/ppermute | solution.py:25
  55.5 13.4 %collective-permute-start.9 = (bf16[2,128,128]{2,1,0:T(8,128)(2,1)S(1)}, bf16[2,128,128]{2,1,0:T(8,128)(2,1)S(1)}, u32[]{:S(2)}, u32[]{:S(2)}) collective-permute-start(bf16[2,128,128]{2,1,0:T(8,128)(2,1)S(1)} %get-tuple-element.14), channel_id=1, source_target_pairs={{64,0},{68,4},{72,8},{76,12},{80,16},{84,20},{88,24},{92,28},{96,3... | collective-permute-start | bytes 196616 | tf_op jit(solution)/shard_map/ppermute | solution.py:25
  56.8 12.2 %collective-permute-start.10 = (bf16[2,128,128]{2,1,0:T(8,128)(2,1)S(1)}, bf16[2,128,128]{2,1,0:T(8,128)(2,1)S(1)}, u32[]{:S(2)}, u32[]{:S(2)}) collective-permute-start(bf16[2,128,128]{2,1,0:T(8,128)(2,1)S(1)} %get-tuple-element.13), channel_id=1, source_target_pairs={{68,0},{72,4},{76,8},{80,12},{84,16},{88,20},{92,24},{96,28},{100,... | collective-permute-start | bytes 196616 | tf_op jit(solution)/shard_map/ppermute | solution.py:25
  102.4 21.2 %copy-start.7 = (f32[32,1152]{1,0:T(8,128)S(1)}, f32[32,1152]{1,0:T(8,128)}, u32[]{:S(2)}) copy-start(f32[32,1152]{1,0:T(8,128)} %reduce-scatter.2.cloned.1.call-done) | copy-start | bytes 442372
Sparse Core Ops, SparseCore 0:
  70.7 31.6 reduce-scatter.1
